TPU v7x, 512 devices: a whole 4x4x16 slice. The times are simulated.
512 devices in a mesh: bond: 32 (over z, core), row: 16 (over y, x).
Axes of the slice: x: 4, y: 4, z: 16, core: 2. Of those that a mesh axis runs over, the one named last changes fastest.
Arguments:
- left_core: float32 [32, 384, 2, 384], P('bond', 'row'), may hold values from -1 to 2
- right_core: float32 [32, 384, 2, 384], P('bond', 'row'), may hold values from -1 to 2
- gate_angles: float32 [32, 6], P('bond'), may hold values from -3.140625 to 3.140625
- sketch: float32 [768, 384], P('bond'), may hold values from -0.21875 to 0.21875
Outputs:
- next_pair: float32 [32, 768, 768], P('bond', 'row')
All inputs are finite; a program needn't handle non-finite values.
Results may differ from a plain program's by a relative error of at most 0.0003.
Values sent between devices are 32-bit elements; how exact they have to be, the bound alone decides.
No kernel may reach another device: no remote copies, remote signals or barrier semaphores. Data moves between devices by JAX's collectives and lax.ppermute only.
A program may use at most 64 MiB of HBM per device.

v0:
```python
import jax
import jax.numpy as jnp
import numpy as np
from jax import lax
from jax.sharding import PartitionSpec as P

ITERS = 2
HIGHEST = lax.Precision.HIGHEST
PLANES = ((0, 1), (2, 3), (0, 2), (1, 3), (0, 3), (1, 2))


def from_behind(value, axis, steps):
    count = lax.axis_size(axis)
    initial, last = (max(0, -steps), min(count, count - steps))
    return lax.ppermute(value, axis, [(source, source + steps) for source in range(initial, last)])


def rotation(first_axis, second_axis, cosine, sine_value):
    unit = np.eye(4, dtype=np.float32)
    diag_part = np.outer(unit[first_axis], unit[first_axis]) + np.outer(
        unit[second_axis], unit[second_axis]
    )
    skew_part = np.outer(unit[second_axis], unit[first_axis]) - np.outer(
        unit[first_axis], unit[second_axis]
    )
    rest_part = np.eye(4, dtype=np.float32) - diag_part
    return (
        jnp.asarray(rest_part)
        + cosine * jnp.asarray(diag_part)
        + sine_value * jnp.asarray(skew_part)
    )


def build_gate(angles):
    gate_matrix = jnp.eye(4, dtype=jnp.float32)
    for number, plane in enumerate(PLANES):
        rotated = rotation(plane[0], plane[1], jnp.cos(angles[number]), jnp.sin(angles[number]))
        gate_matrix = jnp.dot(
            rotated, gate_matrix, precision=HIGHEST, preferred_element_type=jnp.float32
        )
    return gate_matrix


def apply_gate(two_site, gate_matrix):
    width = two_site.shape[1] // 2
    blocks = two_site.reshape(two_site.shape[0] // 2, 2, 2, width)
    mixed_gate = jnp.einsum(
        "pqtu,atuc->apqc", gate_matrix.reshape(2, 2, 2, 2), blocks, precision=HIGHEST
    )
    return mixed_gate.reshape(two_site.shape)


def matmul(left_side, right_side):
    return jnp.dot(left_side, right_side, precision=HIGHEST, preferred_element_type=jnp.float32)


def inner_rows(left_side, right_side):
    return lax.dot_general(
        left_side,
        right_side,
        (((0,), (0,)), ((), ())),
        precision=HIGHEST,
        preferred_element_type=jnp.float32,
    )


def orthonormal(sketched):
    gram_matrix = lax.psum(inner_rows(sketched, sketched), "row")
    chol_factor = jnp.linalg.cholesky(gram_matrix)
    return lax.linalg.triangular_solve(
        chol_factor, sketched, left_side=False, lower=True, transpose_a=True
    )


def on_device(left_core, right_core, gate_angles, sketch):
    width = left_core.shape[3]
    local_sites = left_core.shape[1]
    local_rows = 2 * local_sites
    left_matrix = left_core.reshape(local_rows, width)
    shard_part = lax.all_gather(right_core, "row", axis=1, tiled=True)
    count = shard_part.shape[1]
    two_site = matmul(left_matrix, shard_part.reshape(count, 2 * width))
    two_site = apply_gate(two_site, build_gate(gate_angles[0]))
    shard_part = lax.all_gather(sketch, "bond", axis=0, tiled=True)
    sketched = matmul(two_site, shard_part)
    ortho_basis = orthonormal(sketched)
    for repeat in range(ITERS):
        projected = lax.psum(inner_rows(two_site, ortho_basis), "row")
        ortho_basis = orthonormal(matmul(two_site, projected))
    carried = lax.psum_scatter(
        inner_rows(ortho_basis, two_site), "row", scatter_dimension=0, tiled=True
    )
    incoming = from_behind(carried, "bond", 1)
    incoming_matrix = incoming.reshape(local_rows, width)
    stacked_final = ortho_basis.reshape(local_sites, 2, width)
    shard_part = lax.all_gather(stacked_final, "row", axis=0, tiled=True)
    count = shard_part.shape[0]
    next_block = matmul(incoming_matrix, shard_part.reshape(count, 2 * width))
    return next_block[None]


def solution(mesh):
    return jax.shard_map(
        on_device,
        mesh=mesh,
        in_specs=(
            P("bond", "row", None, None),
            P("bond", "row", None, None),
            P("bond", None),
            P("bond", None),
        ),
        out_specs=P("bond", "row", None),
        check_vma=False,
    )
```

profile of v0, /device:TPU:2, one launch (start us, length us, event | category | flops | bytes accessed | tf_op | source)
XLA Modules:
  0.0 1195.2 jit_solution(12344548351591145168)
XLA Ops:
  23.2 49.4 %all-gather.4.cloned.1.call-done = f32[1,384,2,384]{3,2,0,1:T(2,128)} async-done(((f32[1,24,2,384]{3,2,0,1:T(2,128)}), f32[1,384,2,384]{3,2,0,1:T(2,128)}) %all-gather.4.cloned.1.call-update) | async-done | bytes 1179664 | tf_op jit(solution)/shard_map/all_gather | solution.py:80
  76.4 68.8 %all-gather.6.cloned.1.call-done = f32[768,384]{1,0:T(8,128)} async-done(((f32[24,384]{1,0:T(8,128)}), f32[768,384]{1,0:T(8,128)}) %all-gather.6.cloned.1.call-update) | async-done | bytes 1179664 | tf_op jit(solution)/shard_map/all_gather | solution.py:84
  149.2 112.5 %all-reduce.8.cloned.1.call-done = f32[384,384]{0,1:T(8,128)} async-done(((f32[384,384]{0,1:T(8,128)}), f32[384,384]{0,1:T(8,128)}) %all-reduce.8.cloned.1.call-update) | async-done | bytes 589840 | tf_op jit(solution)/shard_map/psum | solution.py:68
  263.2 11.7 cholesky.273
  285.4 11.7 cholesky.292
  297.2 9.9 custom-call.24
  307.6 11.7 cholesky.311
  328.8 29.5 %custom-call.25 = f32[3,128,128]{1,2,0:T(8,128)S(1)} custom-call(f32[3,128,128]{2,1,0:T(8,128)S(1)} %get-tuple-element.27), custom_call_target="InvertDiagBlocksLowerTriangular" | custom-call | tf_op jit(solution)/shard_map/triangular_solve/custom-call.2 | solution.py:70
  361.6 117.3 %all-reduce.10.cloned.1.call-done = f32[768,384]{1,0:T(8,128)} async-done(((f32[768,384]{1,0:T(8,128)}), f32[768,384]{1,0:T(8,128)}) %all-reduce.10.cloned.1.call-update) | async-done | bytes 1179664 | tf_op jit(solution)/shard_map/psum | solution.py:88
  482.6 115.5 %all-reduce.12.cloned.1.call-done = f32[384,384]{0,1:T(8,128)} async-done(((f32[384,384]{0,1:T(8,128)}), f32[384,384]{0,1:T(8,128)}) %all-reduce.12.cloned.1.call-update) | async-done | bytes 589840 | tf_op jit(solution)/shard_map/psum | solution.py:68
  599.6 11.7 cholesky.326
  621.8 11.7 cholesky.345
  633.5 10.2 custom-call.27
  644.2 11.7 cholesky.364
  666.0 29.5 %custom-call.28 = f32[3,128,128]{1,2,0:T(8,128)S(1)} custom-call(f32[3,128,128]{2,1,0:T(8,128)S(1)} %get-tuple-element.28), custom_call_target="InvertDiagBlocksLowerTriangular" | custom-call | tf_op jit(solution)/shard_map/triangular_solve/custom-call.2 | solution.py:70
  698.8 117.3 %all-reduce.14.cloned.1.call-done = f32[768,384]{1,0:T(8,128)} async-done(((f32[768,384]{1,0:T(8,128)}), f32[768,384]{1,0:T(8,128)}) %all-reduce.14.cloned.1.call-update) | async-done | bytes 1179664 | tf_op jit(solution)/shard_map/psum | solution.py:88
  819.8 115.5 %all-reduce.16.cloned.1.call-done = f32[384,384]{0,1:T(8,128)} async-done(((f32[384,384]{0,1:T(8,128)}), f32[384,384]{0,1:T(8,128)}) %all-reduce.16.cloned.1.call-update) | async-done | bytes 589840 | tf_op jit(solution)/shard_map/psum | solution.py:68
  936.8 11.7 cholesky.379
  959.0 11.7 cholesky.398
  970.7 10.0 custom-call.30
  981.2 11.7 cholesky.417
  1003.0 29.5 %custom-call.31 = f32[3,128,128]{1,2,0:T(8,128)S(1)} custom-call(f32[3,128,128]{2,1,0:T(8,128)S(1)} %get-tuple-element.29), custom_call_target="InvertDiagBlocksLowerTriangular" | custom-call | tf_op jit(solution)/shard_map/triangular_solve/custom-call.2 | solution.py:70
  1036.5 88.4 %reduce-scatter.4.cloned.1.call-done = f32[24,768]{1,0:T(8,128)} async-done(((f32[384,768]{1,0:T(8,128)}), f32[24,768]{1,0:T(8,128)}) %reduce-scatter.4.cloned.1.call-update) | async-done | bytes 73744
  1126.2 59.4 %all-gather.8.cloned.1.call-done = f32[384,2,384]{2,1,0:T(2,128)} async-done(((f32[24,2,384]{2,1,0:T(2,128)}), f32[384,2,384]{2,1,0:T(2,128)}) %all-gather.8.cloned.1.call-update) | async-done | bytes 1179664 | tf_op jit(solution)/shard_map/all_gather | solution.py:96
  (155 shorter events, 117.2 us)
Async XLA Ops:
  6.5 66.1 %all-gather.4.cloned.1.call-start = ((), (), s32[]{:S(2)}) async-start(), calls=%async_computation.1 | async-start | bytes 1253376 | tf_op jit(solution)/shard_map/all_gather | solution.py:80
  7.3 138.0 %all-gather.6.cloned.1.call-start = ((), (), s32[]{:S(2)}) async-start(), calls=%async_computation.2 | async-start | bytes 1216512 | tf_op jit(solution)/shard_map/all_gather | solution.py:84
  8.0 253.8 %all-reduce.8.cloned.1.call-start = ((), (), s32[]{:S(2)}) async-start(), calls=%async_computation.3 | async-start | bytes 1179648 | tf_op jit(solution)/shard_map/psum | solution.py:68
  74.0 0.9 copy-start.3
  148.7 330.2 %all-reduce.10.cloned.1.call-start = ((), (), s32[]{:S(2)}) async-start(), calls=%async_computation.4 | async-start | bytes 2359296 | tf_op jit(solution)/shard_map/psum | solution.py:88
  261.8 1.4 copy-start
  361.6 236.5 %all-reduce.12.cloned.1.call-start = ((), (), s32[]{:S(2)}) async-start(), calls=%async_computation.5 | async-start | bytes 1179648 | tf_op jit(solution)/shard_map/psum | solution.py:68
  482.4 333.7 %all-reduce.14.cloned.1.call-start = ((), (), s32[]{:S(2)}) async-start(), calls=%async_computation.6 | async-start | bytes 2359296 | tf_op jit(solution)/shard_map/psum | solution.py:88
  598.1 1.4 copy-start.1
  698.8 236.5 %all-reduce.16.cloned.1.call-start = ((), (), s32[]{:S(2)}) async-start(), calls=%async_computation.7 | async-start | bytes 1179648 | tf_op jit(solution)/shard_map/psum | solution.py:68
  819.6 305.3 %reduce-scatter.4.cloned.1.call-start = ((), (), s32[]{:S(2)}) async-start(), calls=%async_computation.9 | async-start | bytes 1253376
  935.3 1.4 copy-start.2
  1035.7 149.8 %all-gather.8.cloned.1.call-start = ((), (), s32[]{:S(2)}) async-start(), calls=%async_computation.8 | async-start | bytes 1253376 | tf_op jit(solution)/shard_map/all_gather | solution.py:96
  1124.9 62.0 %collective-permute-start = (f32[24,768]{1,0:T(8,128)}, f32[24,768]{1,0:T(8,128)S(1)}, u32[]{:S(2)}, u32[]{:S(2)}) collective-permute-start(f32[24,768]{1,0:T(8,128)} %reduce-scatter.4.cloned.1.call-done), channel_id=1, source_target_pairs={{0,16},{16,32},{32,48},{48,64},{64,80},{80,96},{96,112},{112,128},... | collective-permute-start | bytes 221192 | tf_op jit(solution)/shard_map/ppermute | solution.py:15
Sparse Core Ops, SparseCore 0:
  10.3 62.2 all-gather.3
  74.8 70.3 all-gather.5
  148.8 112.8 all-reduce.7
  361.7 117.1 all-reduce.9
  482.5 115.5 all-reduce.11
  698.9 117.1 all-reduce.13
  819.7 115.5 all-reduce.15
  1035.8 88.9 reduce-scatter.3
  1127.9 57.6 all-gather.7
where the time goes:
time: 1200 us
  waiting for transfers between devices  846 us (70%)
  other arithmetic  259 us (22%)
  matrix products  31.1 us (3%)
  local copies, waits for them, and re-layouts  28.3 us (2%)
  between operations  28.1 us (2%)
    psum x3, waiting for transfers between devices, orthonormal(): gram_matrix = lax.psum(inner_rows(sketched, sketched), 'row')  344 us
    psum x2, waiting for transfers between devices, on_device(): projected = lax.psum(inner_rows(two_site, ortho_basis), 'row')  235 us
    another operation x32, other arithmetic, orthonormal(): chol_factor = jnp.linalg.cholesky(gram_matrix)  171 us
    unnamed x10, waiting for transfers between devices  89.9 us
    another operation x8, other arithmetic, orthonormal(): lax.linalg.triangular_solve(chol_factor, sketched, left_side=False, lower...  88.6 us
    all_gather x1, waiting for transfers between devices, on_device(): shard_part = lax.all_gather(sketch, 'bond', axis=0, tiled=True)  68.8 us
    all_gather x1, waiting for transfers between devices, on_device(): shard_part = lax.all_gather(stacked_final, 'row', axis=0, tiled=True)  59.4 us
    all_gather x1, waiting for transfers between devices, on_device(): shard_part = lax.all_gather(right_core, 'row', axis=1, tiled=True)  49.4 us
  transfers between devices with their start and end apart: 10, of which 9 were waited for; matrix products, arithmetic and copies ran while one was open for 1% of the time, Pallas kernels for 0%

commit v1 on v0

--- a/solution.py
+++ b/solution.py
@@ -77,7 +77,8 @@
     local_sites = left_core.shape[1]
     local_rows = 2 * local_sites
     left_matrix = left_core.reshape(local_rows, width)
-    shard_part = lax.all_gather(right_core, "row", axis=1, tiled=True)
+    outgoing = jnp.stack([right_core] * lax.axis_size("row"))
+    shard_part = jnp.concatenate(lax.all_to_all(outgoing, "row", 0, 0), axis=1)
     count = shard_part.shape[1]
     two_site = matmul(left_matrix, shard_part.reshape(count, 2 * width))
     two_site = apply_gate(two_site, build_gate(gate_angles[0]))

time: 1200 us -> 1140 us (0.950)
  waiting for transfers between devices: 846 us -> 780 us
    all_gather x1 -> x0, waiting for transfers between devices: 49.4 us -> none  [on_device(): shard_part = lax.all_gather(right_core, 'row', axis=1, tiled=True)]
    all_gather x1, waiting for transfers between devices: 68.8 us -> 47.1 us  [on_device(): shard_part = lax.all_gather(sketch, 'bond', axis=0, tiled=True)]
    unnamed x10 -> x9, waiting for transfers between devices: 89.9 us -> 89.2 us
where the time goes in v1:
time: 1140 us
  waiting for transfers between devices  780 us (68%)
  other arithmetic  259 us (23%)
  between operations  28.6 us (3%)
  local copies, waits for them, and re-layouts  28.5 us (2%)
  matrix products  26.8 us (2%)
  starting transfers between devices  11.9 us (1%)
    psum x3, waiting for transfers between devices, orthonormal(): gram_matrix = lax.psum(inner_rows(sketched, sketched), 'row')  344 us
    psum x2, waiting for transfers between devices, on_device(): projected = lax.psum(inner_rows(two_site, ortho_basis), 'row')  235 us
    another operation x32, other arithmetic, orthonormal(): chol_factor = jnp.linalg.cholesky(gram_matrix)  171 us
    unnamed x9, waiting for transfers between devices  89.2 us
    another operation x8, other arithmetic, orthonormal(): lax.linalg.triangular_solve(chol_factor, sketched, left_side=False, lower...  88.6 us
    all_gather x1, waiting for transfers between devices, on_device(): shard_part = lax.all_gather(stacked_final, 'row', axis=0, tiled=True)  59.4 us
    all_gather x1, waiting for transfers between devices, on_device(): shard_part = lax.all_gather(sketch, 'bond', axis=0, tiled=True)  47.1 us
  transfers between devices with their start and end apart: 10, of which 9 were waited for; matrix products, arithmetic and copies ran while one was open for 1% of the time, Pallas kernels for 0%

profile of v1, /device:TPU:2, one launch (start us, length us, event | category | flops | bytes accessed | tf_op | source)
XLA Modules:
  0.0 1135.0 jit_solution(15881413571283322217)
XLA Ops:
  37.5 47.1 %all-gather.3.cloned.1.call-done = f32[768,384]{1,0:T(8,128)} async-done(((f32[24,384]{1,0:T(8,128)}), f32[768,384]{1,0:T(8,128)}) %all-gather.3.cloned.1.call-update) | async-done | bytes 1179664 | tf_op jit(solution)/shard_map/all_gather | solution.py:85
  88.7 112.6 %all-reduce.8.cloned.1.call-done = f32[384,384]{0,1:T(8,128)} async-done(((f32[384,384]{0,1:T(8,128)}), f32[384,384]{0,1:T(8,128)}) %all-reduce.8.cloned.1.call-update) | async-done | bytes 589840 | tf_op jit(solution)/shard_map/psum | solution.py:68
  202.8 11.7 %cholesky.273 = f32[128,128]{1,0:T(8,128)S(1)} custom-call(f32[128,128]{1,0:T(8,128)S(1)} %cholesky.428), custom_call_target="Cholesky" | custom-call | tf_op jit(solution)/shard_map/jit(cholesky)/cholesky | solution.py:69
  214.6 9.8 custom-call.23
  224.9 11.7 %cholesky.292 = f32[128,128]{1,0:T(8,128)S(1)} custom-call(f32[128,128]{1,0:T(8,128)S(1)} %cholesky.432), custom_call_target="Cholesky" | custom-call | tf_op jit(solution)/shard_map/jit(cholesky)/cholesky | solution.py:69
  236.7 9.9 custom-call.24
  247.1 11.7 %cholesky.311 = f32[128,128]{1,0:T(8,128)S(1)} custom-call(f32[128,128]{1,0:T(8,128)S(1)} %convolution_subtract_fusion.5), custom_call_target="Cholesky" | custom-call | tf_op jit(solution)/shard_map/jit(cholesky)/cholesky | solution.py:69
  268.4 29.5 %custom-call.25 = f32[3,128,128]{1,2,0:T(8,128)S(1)} custom-call(f32[3,128,128]{2,1,0:T(8,128)S(1)} %get-tuple-element.27), custom_call_target="InvertDiagBlocksLowerTriangular" | custom-call | tf_op jit(solution)/shard_map/triangular_solve/custom-call.2 | solution.py:70
  301.2 117.3 %all-reduce.10.cloned.1.call-done = f32[768,384]{1,0:T(8,128)} async-done(((f32[768,384]{1,0:T(8,128)}), f32[768,384]{1,0:T(8,128)}) %all-reduce.10.cloned.1.call-update) | async-done | bytes 1179664 | tf_op jit(solution)/shard_map/psum | solution.py:89
  422.2 115.5 %all-reduce.12.cloned.1.call-done = f32[384,384]{0,1:T(8,128)} async-done(((f32[384,384]{0,1:T(8,128)}), f32[384,384]{0,1:T(8,128)}) %all-reduce.12.cloned.1.call-update) | async-done | bytes 589840 | tf_op jit(solution)/shard_map/psum | solution.py:68
  539.1 11.7 %cholesky.326 = f32[128,128]{1,0:T(8,128)S(1)} custom-call(f32[128,128]{1,0:T(8,128)S(1)} %cholesky.436), custom_call_target="Cholesky" | custom-call | tf_op jit(solution)/shard_map/jit(cholesky)/cholesky | solution.py:69
  561.3 11.7 %cholesky.345 = f32[128,128]{1,0:T(8,128)S(1)} custom-call(f32[128,128]{1,0:T(8,128)S(1)} %cholesky.440), custom_call_target="Cholesky" | custom-call | tf_op jit(solution)/shard_map/jit(cholesky)/cholesky | solution.py:69
  573.0 10.2 custom-call.27
  583.7 11.7 %cholesky.364 = f32[128,128]{1,0:T(8,128)S(1)} custom-call(f32[128,128]{1,0:T(8,128)S(1)} %convolution_subtract_fusion.4), custom_call_target="Cholesky" | custom-call | tf_op jit(solution)/shard_map/jit(cholesky)/cholesky | solution.py:69
  605.6 29.5 %custom-call.28 = f32[3,128,128]{1,2,0:T(8,128)S(1)} custom-call(f32[3,128,128]{2,1,0:T(8,128)S(1)} %get-tuple-element.28), custom_call_target="InvertDiagBlocksLowerTriangular" | custom-call | tf_op jit(solution)/shard_map/triangular_solve/custom-call.2 | solution.py:70
  638.4 117.3 %all-reduce.14.cloned.1.call-done = f32[768,384]{1,0:T(8,128)} async-done(((f32[768,384]{1,0:T(8,128)}), f32[768,384]{1,0:T(8,128)}) %all-reduce.14.cloned.1.call-update) | async-done | bytes 1179664 | tf_op jit(solution)/shard_map/psum | solution.py:89
  759.3 115.5 %all-reduce.16.cloned.1.call-done = f32[384,384]{0,1:T(8,128)} async-done(((f32[384,384]{0,1:T(8,128)}), f32[384,384]{0,1:T(8,128)}) %all-reduce.16.cloned.1.call-update) | async-done | bytes 589840 | tf_op jit(solution)/shard_map/psum | solution.py:68
  876.3 11.7 %cholesky.379 = f32[128,128]{1,0:T(8,128)S(1)} custom-call(f32[128,128]{1,0:T(8,128)S(1)} %cholesky.444), custom_call_target="Cholesky" | custom-call | tf_op jit(solution)/shard_map/jit(cholesky)/cholesky | solution.py:69
  898.5 11.7 %cholesky.398 = f32[128,128]{1,0:T(8,128)S(1)} custom-call(f32[128,128]{1,0:T(8,128)S(1)} %cholesky.448), custom_call_target="Cholesky" | custom-call | tf_op jit(solution)/shard_map/jit(cholesky)/cholesky | solution.py:69
  910.2 10.0 custom-call.30
  920.7 11.7 %cholesky.417 = f32[128,128]{1,0:T(8,128)S(1)} custom-call(f32[128,128]{1,0:T(8,128)S(1)} %convolution_subtract_fusion.3), custom_call_target="Cholesky" | custom-call | tf_op jit(solution)/shard_map/jit(cholesky)/cholesky | solution.py:69
  942.6 29.5 %custom-call.31 = f32[3,128,128]{1,2,0:T(8,128)S(1)} custom-call(f32[3,128,128]{2,1,0:T(8,128)S(1)} %get-tuple-element.29), custom_call_target="InvertDiagBlocksLowerTriangular" | custom-call | tf_op jit(solution)/shard_map/triangular_solve/custom-call.2 | solution.py:70
  976.0 88.4 %reduce-scatter.4.cloned.1.call-done = f32[24,768]{1,0:T(8,128)} async-done(((f32[384,768]{1,0:T(8,128)}), f32[24,768]{1,0:T(8,128)}) %reduce-scatter.4.cloned.1.call-update) | async-done | bytes 73744
  1065.7 59.4 %all-gather.5.cloned.1.call-done = f32[384,2,384]{2,1,0:T(2,128)} async-done(((f32[24,2,384]{2,1,0:T(2,128)}), f32[384,2,384]{2,1,0:T(2,128)}) %all-gather.5.cloned.1.call-update) | async-done | bytes 1179664 | tf_op jit(solution)/shard_map/all_gather | solution.py:97
  (181 shorter events, 117.8 us)
Async XLA Ops:
  6.5 78.1 %all-gather.3.cloned.1.call-start = ((), (), s32[]{:S(2)}) async-start(), calls=%async_computation.2 | async-start | bytes 1216512 | tf_op jit(solution)/shard_map/all_gather | solution.py:85
  9.5 9.7 copy-start.4
  9.5 18.8 %copy-start.9 = (f32[4,4]{1,0:T(4,128)S(1)}, f32[4,4]{1,0:T(4,128)}, u32[]{:S(2)}) copy-start(f32[4,4]{1,0:T(4,128)} %constant.102.clone) | copy-start | bytes 196
  9.5 18.8 %copy-start.10 = (f32[4,4]{1,0:T(4,128)S(1)}, f32[4,4]{1,0:T(4,128)}, u32[]{:S(2)}) copy-start(f32[4,4]{1,0:T(4,128)} %constant.103.clone) | copy-start | bytes 196
  9.5 18.8 %copy-start.16 = (f32[4,4]{1,0:T(4,128)S(1)}, f32[4,4]{1,0:T(4,128)}, u32[]{:S(2)}) copy-start(f32[4,4]{1,0:T(4,128)} %constant.104.clone) | copy-start | bytes 196
  9.5 18.9 %copy-start.15 = (f32[4,4]{1,0:T(4,128)S(1)}, f32[4,4]{1,0:T(4,128)}, u32[]{:S(2)}) copy-start(f32[4,4]{1,0:T(4,128)} %constant.105.clone) | copy-start | bytes 196
  9.5 19.1 %copy-start.7 = (f32[4,4]{1,0:T(4,128)S(1)}, f32[4,4]{1,0:T(4,128)}, u32[]{:S(2)}) copy-start(f32[4,4]{1,0:T(4,128)} %constant.106.clone) | copy-start | bytes 196
  9.5 19.1 %copy-start.8 = (f32[4,4]{1,0:T(4,128)S(1)}, f32[4,4]{1,0:T(4,128)}, u32[]{:S(2)}) copy-start(f32[4,4]{1,0:T(4,128)} %constant.107.clone) | copy-start | bytes 196
  9.5 19.1 %copy-start.14 = (f32[4,4]{1,0:T(4,128)S(1)}, f32[4,4]{1,0:T(4,128)}, u32[]{:S(2)}) copy-start(f32[4,4]{1,0:T(4,128)} %constant.108.clone) | copy-start | bytes 196
  9.6 19.2 %copy-start.13 = (f32[4,4]{1,0:T(4,128)S(1)}, f32[4,4]{1,0:T(4,128)}, u32[]{:S(2)}) copy-start(f32[4,4]{1,0:T(4,128)} %constant.109.clone) | copy-start | bytes 196
  9.6 19.3 %copy-start.5 = (f32[4,4]{1,0:T(4,128)S(1)}, f32[4,4]{1,0:T(4,128)}, u32[]{:S(2)}) copy-start(f32[4,4]{1,0:T(4,128)} %constant.110.clone) | copy-start | bytes 196
  9.6 19.3 %copy-start.6 = (f32[4,4]{1,0:T(4,128)S(1)}, f32[4,4]{1,0:T(4,128)}, u32[]{:S(2)}) copy-start(f32[4,4]{1,0:T(4,128)} %constant.111.clone) | copy-start | bytes 196
  9.6 19.3 %copy-start.12 = (f32[4,4]{1,0:T(4,128)S(1)}, f32[4,4]{1,0:T(4,128)}, u32[]{:S(2)}) copy-start(f32[4,4]{1,0:T(4,128)} %constant.112.clone) | copy-start | bytes 196
  9.6 19.4 %copy-start.11 = (f32[4,4]{1,0:T(4,128)S(1)}, f32[4,4]{1,0:T(4,128)}, u32[]{:S(2)}) copy-start(f32[4,4]{1,0:T(4,128)} %constant.113.clone) | copy-start | bytes 196
  9.6 25.4 %all-to-all-start = ((f32[16,1,24,2,384]{4,3,2,1,0:T(2,128)}), f32[16,1,24,2,384]{4,3,2,1,0:T(2,128)S(1)}, u32[]{:S(2)}, u32[]{:S(2)}) async-start(f32[16,1,24,2,384]{4,3,2,1,0:T(2,128)} %stack.2), calls=%async_computation | async-start | bytes 2359296 | tf_op jit(solution)/shard_map/all_to_all | solution.py:81
  19.1 182.2 %all-reduce.8.cloned.1.call-start = ((), (), s32[]{:S(2)}) async-start(), calls=%async_computation.3 | async-start | bytes 1179648 | tf_op jit(solution)/shard_map/psum | solution.py:68
  88.1 330.3 %all-reduce.10.cloned.1.call-start = ((), (), s32[]{:S(2)}) async-start(), calls=%async_computation.4 | async-start | bytes 2359296 | tf_op jit(solution)/shard_map/psum | solution.py:89
  201.3 1.4 copy-start
  301.1 236.5 %all-reduce.12.cloned.1.call-start = ((), (), s32[]{:S(2)}) async-start(), calls=%async_computation.5 | async-start | bytes 1179648 | tf_op jit(solution)/shard_map/psum | solution.py:68
  421.9 333.7 %all-reduce.14.cloned.1.call-start = ((), (), s32[]{:S(2)}) async-start(), calls=%async_computation.6 | async-start | bytes 2359296 | tf_op jit(solution)/shard_map/psum | solution.py:89
  638.3 236.5 %all-reduce.16.cloned.1.call-start = ((), (), s32[]{:S(2)}) async-start(), calls=%async_computation.7 | async-start | bytes 1179648 | tf_op jit(solution)/shard_map/psum | solution.py:68
  759.1 305.3 %reduce-scatter.4.cloned.1.call-start = ((), (), s32[]{:S(2)}) async-start(), calls=%async_computation.9 | async-start | bytes 1253376
  975.3 149.8 %all-gather.5.cloned.1.call-start = ((), (), s32[]{:S(2)}) async-start(), calls=%async_computation.8 | async-start | bytes 1253376 | tf_op jit(solution)/shard_map/all_gather | solution.py:97
  1064.4 62.0 %collective-permute-start = (f32[24,768]{1,0:T(8,128)}, f32[24,768]{1,0:T(8,128)S(1)}, u32[]{:S(2)}, u32[]{:S(2)}) collective-permute-start(f32[24,768]{1,0:T(8,128)} %reduce-scatter.4.cloned.1.call-done), channel_id=1, source_target_pairs={{0,16},{16,32},{32,48},{48,64},{64,80},{80,96},{96,112},{112,128},... | collective-permute-start | bytes 221192 | tf_op jit(solution)/shard_map/ppermute | solution.py:15
  (3 other events, 3.6 us)
Sparse Core Ops, SparseCore 0:
  9.5 75.1 all-gather.2
  88.2 113.0 all-reduce.7
  301.2 117.1 all-reduce.9
  422.0 115.5 all-reduce.11
  638.4 117.1 all-reduce.13
  759.2 115.5 all-reduce.15
  975.4 88.9 reduce-scatter.3
  1067.4 57.6 all-gather.4
